TPU v7x, 128 devices: a whole 4x4x4 slice. The times are simulated.
128 devices in a mesh: wide: 16 (over y_hi, z, core), blk: 8 (over x, y_lo).
Axes of the slice: x: 4, y: 4 (y_hi: 2, y_lo: 2; y = y_hi * 2 + y_lo), z: 4, core: 2. Of those that a mesh axis runs over, the one named last changes fastest.
Arguments:
- queries: bfloat16 [512, 64, 512], P(('wide', 'blk')), may hold values from -6 to 6
- references: bfloat16 [256, 64, 512], P(('wide', 'blk')), may hold values from -6 to 6
- query_taps: bfloat16 [16, 9], replicated, may hold values from -2 to 2
- ref_taps: bfloat16 [16, 9], replicated, may hold values from -0.5 to 0.5
- tap_bias: float32 [16], replicated, may hold values from -3 to 3
- candidates: int32 [128, 16], P(('wide', 'blk')), may hold values 0 or 1
Outputs:
- scores: float32 [512, 256], P(('wide', 'blk'))
All inputs are finite; a program needn't handle non-finite values. No bound on the sum of `candidates` on one device may be relied on, other than what follows from the above.
Results may differ from a plain program's by a relative error of at most 0.0006.
Values may be sent and summed in bfloat16 or wider, within the bound.
No kernel may reach another device: no remote copies, remote signals or barrier semaphores. Data moves between devices by JAX's collectives and lax.ppermute only.
A program may use at most 64 MiB of HBM per device.

v0:
```python
import math

import jax
import jax.numpy as jnp
from jax import lax
from jax.experimental import pallas as pl
from jax.experimental.pallas import tpu as pltpu
from jax.sharding import PartitionSpec as P

SIDE = 8


epsilon = 1e-06


def conv_table(weights, width):
    count = width * width
    position = jnp.arange(count, dtype=jnp.int32)
    grid_row = position // width
    grid_col = position % width
    delta_row = grid_row[None, :] - grid_row[:, None]
    delta_col = grid_col[None, :] - grid_col[:, None]
    inside = (jnp.abs(delta_row) <= 1) & (jnp.abs(delta_col) <= 1)
    tap_index = (delta_row + 1) * 3 + (delta_col + 1)
    selector = (tap_index[None] == jnp.arange(9, dtype=jnp.int32)[:, None, None]) & inside[None]
    table = jnp.sum(
        jnp.where(selector[None], weights.astype(jnp.float32)[:, :, None, None], jnp.float32(0.0)),
        axis=1,
    )
    return table.astype(jnp.bfloat16)


def normalize(features):
    values = features.astype(jnp.float32)
    inverse_rms = lax.rsqrt(jnp.mean(values * values, axis=-1, keepdims=True) + epsilon)
    return (values * inverse_rms).astype(jnp.bfloat16)


CH = 256


GB = 4


def filter_kernel(idx_ref, cnt_ref, q_ref, r_ref, qt_ref, bias_ref, rtt_ref, col_ref, row_ref,
                  c_scr, h_scr, rt_ref, f_scr):
    t = pl.program_id(0)
    rows = q_ref.shape[0]
    hid = rtt_ref.shape[0]
    cells = rtt_ref.shape[1]
    depth = q_ref.shape[1]
    nq = rows // cells
    r4 = CH // cells
    br = r4 // 2
    groups = col_ref.shape[2] // 2
    scale = math.sqrt(depth)
    per = hid // 4

    @pl.when(t == 0)
    def _():
        rt_ref[...] = jnp.zeros(rt_ref.shape, rt_ref.dtype)
        for k in range(hid):
            blockk = rtt_ref[k]
            for x in range(r4):
                rt_ref[k, x * cells:(x + 1) * cells, x * cells:(x + 1) * cells] = blockk

    qt = q_ref[...]
    for g in range(groups):
        @pl.when(g * GB < cnt_ref[t])
        def _():
            for slot in range(GB):
                blk_id = idx_ref[t, g * GB + slot]
                start = pl.multiple_of(blk_id * (br * cells), br * cells)
                corr = lax.dot_general(
                    qt, r_ref[pl.ds(start, br * cells), :], (((1,), (1,)), ((), ())),
                    preferred_element_type=jnp.float32,
                )
                c_scr[:, slot * br * cells:(slot + 1) * br * cells] = (corr / scale).astype(jnp.bfloat16)
            for p in range(nq):
                for c2 in range(2):
                    cc = c_scr[p * cells:(p + 1) * cells, c2 * CH:(c2 + 1) * CH]
                    for kg in range(hid // per):
                        hq = jnp.dot(
                            qt_ref[kg * per * cells:(kg + 1) * per * cells, :], cc,
                            preferred_element_type=jnp.float32,
                        )
                        hq = jnp.maximum(hq + bias_ref[kg * per * cells:(kg + 1) * per * cells, :], 0.0)
                        hq = hq.astype(jnp.bfloat16)
                        for kk in range(per):
                            k = kg * per + kk
                            row0 = (p * 2 + c2) * cells
                            h_scr[k, row0:row0 + cells, :] = hq[kk * cells:(kk + 1) * cells, :]
            f_scr[...] = jnp.dot(h_scr[0], rt_ref[0], preferred_element_type=jnp.float32)
            for k in range(1, hid):
                f_scr[...] += jnp.dot(h_scr[k], rt_ref[k], preferred_element_type=jnp.float32)
            for p in range(nq):
                acc = f_scr[p * 2 * cells:(p + 1) * 2 * cells, :]
                col_ref[0, p, 2 * g:2 * g + 2, :] = jnp.max(acc.reshape(2, cells, CH), axis=1)
                accT = acc.T
                row_ref[0, p, :, 2 * g * cells:(2 * g + 2) * cells] = jnp.max(
                    accT.reshape(r4, cells, 2 * cells), axis=1)


def local_scores(q_all, r_all, cand, query_table, ref_table, tap_bias):
    tiles = q_all.shape[0]
    depth = q_all.shape[2]
    nrl, cells = r_all.shape[0], r_all.shape[1]
    hid = query_table.shape[0]
    qt_per = 4
    nb = cand.shape[1]
    br = nrl // nb
    chunks = nrl * cells // CH
    r4 = CH // cells
    keep = (cand != 0).astype(jnp.int32)
    idx = jnp.argsort(1 - keep, axis=1, stable=True).astype(jnp.int32)
    cnt = jnp.sum(keep, axis=1).astype(jnp.int32)
    qstack = query_table.reshape(hid * cells, cells)
    bias_col = jnp.repeat(tap_bias.astype(jnp.float32), cells)[:, None]
    rtT = jnp.transpose(ref_table, (0, 2, 1))
    r2 = r_all.reshape(nrl * cells, depth)
    col, row = pl.pallas_call(
        filter_kernel,
        grid_spec=pltpu.PrefetchScalarGridSpec(
            num_scalar_prefetch=2,
            grid=(tiles,),
            in_specs=[
                pl.BlockSpec((None, qt_per * cells, depth), lambda t, i, c: (t, 0, 0)),
                pl.BlockSpec((nrl * cells, depth), lambda t, i, c: (0, 0)),
                pl.BlockSpec((hid * cells, cells), lambda t, i, c: (0, 0)),
                pl.BlockSpec((hid * cells, 1), lambda t, i, c: (0, 0)),
                pl.BlockSpec((hid, cells, cells), lambda t, i, c: (0, 0, 0)),
            ],
            out_specs=[
                pl.BlockSpec((1, qt_per, chunks, CH), lambda t, i, c: (t, 0, 0, 0)),
                pl.BlockSpec((1, qt_per, r4, chunks * cells), lambda t, i, c: (t, 0, 0, 0)),
            ],
            scratch_shapes=[
                pltpu.VMEM((qt_per * cells, GB * br * cells), jnp.bfloat16),
                pltpu.VMEM((hid, qt_per * 2 * cells, CH), jnp.bfloat16),
                pltpu.VMEM((hid, CH, CH), jnp.bfloat16),
                pltpu.VMEM((qt_per * 2 * cells, CH), jnp.float32),
            ],
        ),
        out_shape=[
            jax.ShapeDtypeStruct((tiles, qt_per, chunks, CH), jnp.float32),
            jax.ShapeDtypeStruct((tiles, qt_per, r4, chunks * cells), jnp.float32),
        ],
        compiler_params=pltpu.CompilerParams(vmem_limit_bytes=56 * 1024 * 1024),
    )(idx, cnt, q_all, r2, qstack, bias_col, rtT)
    col_pool = jnp.mean(col.reshape(tiles, qt_per, chunks, r4, cells), axis=-1)
    row_pool = jnp.mean(row.reshape(tiles, qt_per, r4, chunks, cells), axis=-1)
    row_pool = jnp.transpose(row_pool, (0, 1, 3, 2))
    packed = (0.5 * (row_pool + col_pool)).reshape(tiles, qt_per, nb, br)
    where_is = jnp.argsort(idx, axis=1)
    return jnp.take_along_axis(packed, where_is[:, None, :, None], axis=2)


def doubling(x, axis, size):
    bits = size.bit_length() - 1
    for m in reversed(range(bits)):
        other = lax.ppermute(x, axis, [(i, i ^ (1 << m)) for i in range(size)])
        x = jnp.concatenate([x, other], axis=0)
    return x


def bit_reverse(size):
    bits = size.bit_length() - 1
    pos = jnp.arange(size)
    rev = jnp.zeros_like(pos)
    for i in range(bits):
        rev = rev | (((pos >> i) & 1) << (bits - 1 - i))
    return rev


def shards(queries, references, query_taps, ref_taps, tap_bias, candidates):
    query_table = conv_table(query_taps, SIDE)
    ref_table = conv_table(ref_taps, SIDE)
    blk = lax.axis_size("blk")
    wide = lax.axis_size("wide")
    me = lax.axis_index("blk")
    me_w = lax.axis_index("wide")
    query_unit = normalize(queries)
    qt_per, cells, depth = query_unit.shape
    pad = 16
    cand_rows = jnp.zeros((pad, depth), jnp.bfloat16).at[0, :candidates.shape[1]].set(
        candidates[0].astype(jnp.bfloat16))
    payload = jnp.concatenate([query_unit.reshape(qt_per * cells, depth), cand_rows], axis=0)
    q3 = doubling(payload[None], "blk", blk)
    cand = q3[:, qt_per * cells, :candidates.shape[1]]
    b_at = me ^ bit_reverse(blk)
    ref_unit = normalize(references)
    rl = ref_unit.shape[0]
    held = doubling(ref_unit, "wide", wide)
    w_at = me_w ^ bit_reverse(wide)
    cand_pos = jnp.take(cand, w_at, axis=1)
    s = local_scores(q3, held, cand_pos, query_table, ref_table, tap_bias)
    p_of = jnp.argsort(w_at)
    s = jnp.take(s, p_of, axis=2)
    s = jnp.take(s, jnp.argsort(b_at), axis=0)
    mine = lax.all_to_all(s, "blk", 0, 0, tiled=True)
    mine = jnp.transpose(mine, (1, 2, 0, 3)).reshape(qt_per, wide * blk * rl)
    block_refs = blk * rl
    keep = jnp.repeat(candidates[0] != 0, block_refs)
    return jnp.where(keep[None, :], mine, jnp.float32(0.0))


def solution(mesh):
    placed = (
        P(("wide", "blk"), None, None),
        P(("wide", "blk"), None, None),
        P(),
        P(),
        P(),
        P(("wide", "blk"), None),
    )
    return jax.shard_map(
        shards, mesh=mesh, in_specs=placed, out_specs=P(("wide", "blk"), None), check_vma=False
    )
```

profile of v0, /device:TPU:0, one launch (start us, length us, event | category | flops | bytes accessed | tf_op | source)
XLA Modules:
  0.0 149.0 jit_solution(9877969672238185812)
XLA Ops:
  0.0 1.0 fusion.6
  1.0 1.0 constant_dynamic-update-slice_fusion.4
  2.0 3.4 %collective-permute-start.3 = (bf16[2,64,512]{2,1,0:T(8,128)(2,1)S(1)}, bf16[2,64,512]{2,1,0:T(8,128)(2,1)}, u32[]{:S(2)}, u32[]{:S(2)}) collective-permute-start(bf16[2,64,512]{2,1,0:T(8,128)(2,1)S(1)} %get-tuple-element.32), channel_id=1, source_target_pairs={{0,64},{8,72},{16,80},{24,88},{32,96},{40,104},{48,112},{56,120},{... | collective-permute-start | bytes 393224 | tf_op jit(solution)/shard_map/ppermute | solution.py:161
  5.4 1.1 fusion.1
  6.5 1.1 fusion.2
  7.6 0.7 convert_element_type.41
  8.3 3.1 %collective-permute-start = (bf16[1,272,512]{2,1,0:T(8,128)(2,1)S(1)}, bf16[1,272,512]{2,1,0:T(8,128)(2,1)S(1)}, u32[]{:S(2)}, u32[]{:S(2)}) collective-permute-start(bf16[1,272,512]{2,1,0:T(8,128)(2,1)S(1)} %fusion.5), channel_id=1, source_target_pairs={{0,4},{1,5},{2,6},{3,7},{4,0},{5,1},{6,2},{7,3},{8,12},{9,13},{10,... | collective-permute-start | bytes 835592 | tf_op jit(solution)/shard_map/ppermute | solution.py:161
  11.6 1.2 sort.69
  12.8 0.7 convert_element_type.45
  13.5 0.7 convert_element_type.48
  14.3 2.1 %select_reduce_fusion = (bf16[16,64,64]{2,1,0:T(8,128)(2,1)}, bf16[16,64,64]{2,1,0:T(8,128)(2,1)}) fusion(f32[16,9]{1,0:T(8,128)S(1)} %convert_element_type.48, pred[9,64,64]{2,1,0:T(8,128)(4,1)S(1)} %fusion.3, f32[16,9]{1,0:T(8,128)S(1)} %convert_element_type.45), kind=kLoop, calls=%fused_computation.4 | loop fusion | flops 2228224 | bytes 300160 | tf_op jit(solution)/shard_map/reduce_sum | solution.py:26
  16.4 1.5 %collective-permute-done = bf16[1,272,512]{2,1,0:T(8,128)(2,1)S(1)} collective-permute-done((bf16[1,272,512]{2,1,0:T(8,128)(2,1)S(1)}, bf16[1,272,512]{2,1,0:T(8,128)(2,1)S(1)}, u32[]{:S(2)}, u32[]{:S(2)}) %collective-permute-start) | collective-permute-done | bytes 278560 | tf_op jit(solution)/shard_map/ppermute | solution.py:161
  18.0 0.8 pad_maximum_fusion.3
  18.8 1.5 %collective-permute-start.1 = (bf16[2,272,512]{2,1,0:T(8,128)(2,1)}, bf16[2,272,512]{2,1,0:T(8,128)(2,1)S(1)}, u32[]{:S(2)}, u32[]{:S(2)}) collective-permute-start(bf16[2,272,512]{2,1,0:T(8,128)(2,1)} %pad_maximum_fusion.3), channel_id=1, source_target_pairs={{0,2},{1,3},{2,0},{3,1},{4,6},{5,7},{6,4},{7,5},{8,10},{9,11},{10,... | collective-permute-start | bytes 1671176 | tf_op jit(solution)/shard_map/ppermute | solution.py:161
  20.3 1.0 sort.68
  21.3 1.6 %pad_maximum_fusion.5 = bf16[4,64,512]{2,1,0:T(8,128)(2,1)} fusion(bf16[2,64,512]{2,1,0:T(8,128)(2,1)} %collective-permute-done.3, bf16[2,64,512]{2,1,0:T(8,128)(2,1)S(1)} %get-tuple-element.32), kind=kLoop, calls=%fused_computation.25 | loop fusion | flops 131072 | bytes 524288 | tf_op jit(solution)/shard_map/concatenate | solution.py:162
  22.9 3.9 %collective-permute-start.4 = (bf16[4,64,512]{2,1,0:T(8,128)(2,1)}, bf16[4,64,512]{2,1,0:T(8,128)(2,1)S(1)}, u32[]{:S(2)}, u32[]{:S(2)}) collective-permute-start(bf16[4,64,512]{2,1,0:T(8,128)(2,1)} %pad_maximum_fusion.5), channel_id=1, source_target_pairs={{0,32},{8,40},{16,48},{24,56},{32,0},{40,8},{48,16},{56,24},{64,96... | collective-permute-start | bytes 786440 | tf_op jit(solution)/shard_map/ppermute | solution.py:161
  26.8 5.4 %collective-permute-done.1 = bf16[2,272,512]{2,1,0:T(8,128)(2,1)S(1)} collective-permute-done((bf16[2,272,512]{2,1,0:T(8,128)(2,1)}, bf16[2,272,512]{2,1,0:T(8,128)(2,1)S(1)}, u32[]{:S(2)}, u32[]{:S(2)}) %collective-permute-start.1) | collective-permute-done | bytes 557088 | tf_op jit(solution)/shard_map/ppermute | solution.py:161
  32.2 1.1 pad_maximum_fusion.1
  33.3 0.7 collective-permute-start.2
  34.0 1.8 %copy.49 = bf16[16,64,64]{1,2,0:T(8,128)(2,1)} copy(bf16[16,64,64]{2,1,0:T(8,128)(2,1)} %get-tuple-element.29) | data formatting | bytes 262144 | tf_op jit(solution)/shard_map/reduce_sum | solution.py:26
  35.9 1.3 broadcast_in_dim_reshape.5.bias_ref
  37.2 1.0 pad_maximum_fusion.4
  38.2 2.0 %collective-permute-start.5 = (bf16[8,64,512]{2,1,0:T(8,128)(2,1)S(1)}, bf16[8,64,512]{2,1,0:T(8,128)(2,1)S(1)}, u32[]{:S(2)}, u32[]{:S(2)}) collective-permute-start(bf16[8,64,512]{2,1,0:T(8,128)(2,1)S(1)} %pad_maximum_fusion.4), channel_id=1, source_target_pairs={{0,16},{8,24},{16,0},{24,8},{32,48},{40,56},{48,32},{56,40},{64,80... | collective-permute-start | bytes 1572872 | tf_op jit(solution)/shard_map/ppermute | solution.py:161
  40.3 0.9 constant_dynamic-update-slice_fusion.3
  41.2 8.7 %collective-permute-done.5 = bf16[8,64,512]{2,1,0:T(8,128)(2,1)S(1)} collective-permute-done((bf16[8,64,512]{2,1,0:T(8,128)(2,1)S(1)}, bf16[8,64,512]{2,1,0:T(8,128)(2,1)S(1)}, u32[]{:S(2)}, u32[]{:S(2)}) %collective-permute-start.5) | collective-permute-done | bytes 524320 | tf_op jit(solution)/shard_map/ppermute | solution.py:161
  49.9 2.0 %pad_maximum_fusion.2 = bf16[16,64,512]{2,1,0:T(8,128)(2,1)} fusion(bf16[8,64,512]{2,1,0:T(8,128)(2,1)S(1)} %collective-permute-done.5, bf16[4,64,512]{2,1,0:T(8,128)(2,1)S(1)} %collective-permute-done.4, bf16[2,64,512]{2,1,0:T(8,128)(2,1)} %collective-permute-done.3, bf16[2,64,512]{2,1,0:T(8,128)(2,1)} %copy-done.2), kind=kLoop, calls=%fused_computation.8 | loop fusion | flops 1572864 | bytes 2097152 | tf_op jit(solution)/shard_map/concatenate | solution.py:162
  52.0 1.3 copy-done.1
  53.3 4.7 %collective-permute-done.2 = bf16[4,272,512]{2,1,0:T(8,128)(2,1)} collective-permute-done((bf16[4,272,512]{2,1,0:T(8,128)(2,1)}, bf16[4,272,512]{2,1,0:T(8,128)(2,1)}, u32[]{:S(2)}, u32[]{:S(2)}) %collective-permute-start.2) | collective-permute-done | bytes 1114144 | tf_op jit(solution)/shard_map/ppermute | solution.py:161
  58.0 1.5 pad_maximum_fusion.q_ref
  59.6 0.6 gather_fusion
  60.1 0.6 convert_reduce_fusion
  60.7 0.7 sort.70
  61.4 0.7 copy.50.idx_ref
  62.1 0.7 sort.71
  63.0 2.3 %constant_dynamic-update-slice_fusion = bf16[32,64,512]{2,1,0:T(8,128)(2,1)} fusion(bf16[32,64,512]{2,1,0:T(8,128)(2,1)} %copy-done.1, bf16[16,64,512]{2,1,0:T(8,128)(2,1)} %collective-permute-done.6), kind=kLoop, calls=%fused_computation.45 | loop fusion | bytes 2097152 | tf_op jit(solution)/shard_map/concatenate | solution.py:162
  65.3 63.8 %shard_map.64 = (f32[8,4,8,256]{3,2,1,0:T(8,128)}, f32[8,4,4,512]{3,2,1,0:T(4,128)}) custom-call(s32[8,16]{1,0:T(8,128)} %copy.50.idx_ref, s32[8]{0:T(128)} %get-tuple-element.33.cnt_ref, bf16[8,272,512]{2,1,0:T(8,128)(2,1)} %copy-done, bf16[2048,512]{1,0:T(8,128)(2,1)} %bitcast.38, bf16[1024,64]{1,0:T(8,128)(2,1)} %bitcast.40, ...), custom_call_target="tpu_custom_call" | custom-call | tf_op jit(solution)/shard_map/pallas_call | solution.py:121
  129.1 1.2 reshape.341
  130.9 1.2 reshape.340
  132.8 0.9 gather_fusion.3
  134.1 0.6 gather_fusion.1
  134.8 0.6 gather_fusion.2
  135.5 0.7 reshape.382
  136.2 4.4 %all-to-all-start = ((f32[8,1,128]{2,1,0:T(1,128)}), f32[8,1,128]{2,1,0:T(1,128)S(1)}, u32[]{:S(2)}, u32[]{:S(2)}) async-start(f32[8,1,128]{2,1,0:T(1,128)} %reshape.382), calls=%async_computation | async-start | bytes 8192 | tf_op jit(solution)/shard_map/all_to_all | solution.py:200
  140.8 5.9 %all-to-all-done = f32[8,1,128]{2,1,0:T(1,128)S(1)} async-done(((f32[8,1,128]{2,1,0:T(1,128)}), f32[8,1,128]{2,1,0:T(1,128)S(1)}, u32[]{:S(2)}, u32[]{:S(2)}) %all-to-all-start) | async-done | bytes 4128 | tf_op jit(solution)/shard_map/all_to_all | solution.py:200
  146.7 0.5 broadcast.576
  147.2 0.7 reduce.3
  148.3 0.7 copy.60
  (63 shorter events, 3.2 us)
Async XLA Ops:
  2.0 19.3 %copy-start.2 = (bf16[2,64,512]{2,1,0:T(8,128)(2,1)}, bf16[2,64,512]{2,1,0:T(8,128)(2,1)S(1)}, u32[]{:S(2)}) copy-start(bf16[2,64,512]{2,1,0:T(8,128)(2,1)S(1)} %get-tuple-element.32) | copy-start | bytes 393220
  2.0 19.3 %collective-permute-start.3 = (bf16[2,64,512]{2,1,0:T(8,128)(2,1)S(1)}, bf16[2,64,512]{2,1,0:T(8,128)(2,1)}, u32[]{:S(2)}, u32[]{:S(2)}) collective-permute-start(bf16[2,64,512]{2,1,0:T(8,128)(2,1)S(1)} %get-tuple-element.32), channel_id=1, source_target_pairs={{0,64},{8,72},{16,80},{24,88},{32,96},{40,104},{48,112},{56,120},{... | collective-permute-start | bytes 393224 | tf_op jit(solution)/shard_map/ppermute | solution.py:161
  8.3 9.7 %collective-permute-start = (bf16[1,272,512]{2,1,0:T(8,128)(2,1)S(1)}, bf16[1,272,512]{2,1,0:T(8,128)(2,1)S(1)}, u32[]{:S(2)}, u32[]{:S(2)}) collective-permute-start(bf16[1,272,512]{2,1,0:T(8,128)(2,1)S(1)} %fusion.5), channel_id=1, source_target_pairs={{0,4},{1,5},{2,6},{3,7},{4,0},{5,1},{6,2},{7,3},{8,12},{9,13},{10,... | collective-permute-start | bytes 835592 | tf_op jit(solution)/shard_map/ppermute | solution.py:161
  16.4 19.4 %copy-start.3 = (f32[16]{0:T(128)S(1)}, f32[16]{0:T(128)}, u32[]{:S(2)}) copy-start(f32[16]{0:T(128)} %param.12) | copy-start | bytes 196
  18.8 13.4 %collective-permute-start.1 = (bf16[2,272,512]{2,1,0:T(8,128)(2,1)}, bf16[2,272,512]{2,1,0:T(8,128)(2,1)S(1)}, u32[]{:S(2)}, u32[]{:S(2)}) collective-permute-start(bf16[2,272,512]{2,1,0:T(8,128)(2,1)} %pad_maximum_fusion.3), channel_id=1, source_target_pairs={{0,2},{1,3},{2,0},{3,1},{4,6},{5,7},{6,4},{7,5},{8,10},{9,11},{10,... | collective-permute-start | bytes 1671176 | tf_op jit(solution)/shard_map/ppermute | solution.py:161
  22.9 14.3 %collective-permute-start.4 = (bf16[4,64,512]{2,1,0:T(8,128)(2,1)}, bf16[4,64,512]{2,1,0:T(8,128)(2,1)S(1)}, u32[]{:S(2)}, u32[]{:S(2)}) collective-permute-start(bf16[4,64,512]{2,1,0:T(8,128)(2,1)} %pad_maximum_fusion.5), channel_id=1, source_target_pairs={{0,32},{8,40},{16,48},{24,56},{32,0},{40,8},{48,16},{56,24},{64,96... | collective-permute-start | bytes 786440 | tf_op jit(solution)/shard_map/ppermute | solution.py:161
  33.3 24.6 %collective-permute-start.2 = (bf16[4,272,512]{2,1,0:T(8,128)(2,1)}, bf16[4,272,512]{2,1,0:T(8,128)(2,1)}, u32[]{:S(2)}, u32[]{:S(2)}) collective-permute-start(bf16[4,272,512]{2,1,0:T(8,128)(2,1)} %pad_maximum_fusion.1), channel_id=1, source_target_pairs={{0,1},{1,0},{2,3},{3,2},{4,5},{5,4},{6,7},{7,6},{8,9},{9,8},{10,11... | collective-permute-start | bytes 3342344 | tf_op jit(solution)/shard_map/ppermute | solution.py:161
  38.2 11.7 %collective-permute-start.5 = (bf16[8,64,512]{2,1,0:T(8,128)(2,1)S(1)}, bf16[8,64,512]{2,1,0:T(8,128)(2,1)S(1)}, u32[]{:S(2)}, u32[]{:S(2)}) collective-permute-start(bf16[8,64,512]{2,1,0:T(8,128)(2,1)S(1)} %pad_maximum_fusion.4), channel_id=1, source_target_pairs={{0,16},{8,24},{16,0},{24,8},{32,48},{40,56},{48,32},{56,40},{64,80... | collective-permute-start | bytes 1572872 | tf_op jit(solution)/shard_map/ppermute | solution.py:161
  51.9 11.1 %collective-permute-start.6 = (bf16[16,64,512]{2,1,0:T(8,128)(2,1)}, bf16[16,64,512]{2,1,0:T(8,128)(2,1)}, u32[]{:S(2)}, u32[]{:S(2)}) collective-permute-start(bf16[16,64,512]{2,1,0:T(8,128)(2,1)} %pad_maximum_fusion.2), channel_id=1, source_target_pairs={{0,8},{8,0},{16,24},{24,16},{32,40},{40,32},{48,56},{56,48},{64,72... | collective-permute-start | bytes 3145736 | tf_op jit(solution)/shard_map/ppermute | solution.py:161
  52.0 1.3 copy-start.1
  59.4 5.9 %copy-start = (bf16[8,272,512]{2,1,0:T(8,128)(2,1)}, bf16[8,272,512]{2,1,0:T(8,128)(2,1)S(1)}, u32[]{:S(2)}) copy-start(bf16[8,272,512]{2,1,0:T(8,128)(2,1)S(1)} %pad_maximum_fusion.q_ref) | copy-start | bytes 6684676
  130.9 9.7 %copy-start.4 = (s32[1,16]{1,0:T(1,128)S(1)}, s32[1,16]{1,0:T(1,128)}, u32[]{:S(2)}) copy-start(s32[1,16]{1,0:T(1,128)} %param.13) | copy-start | bytes 196
  136.2 10.5 %all-to-all-start = ((f32[8,1,128]{2,1,0:T(1,128)}), f32[8,1,128]{2,1,0:T(1,128)S(1)}, u32[]{:S(2)}, u32[]{:S(2)}) async-start(f32[8,1,128]{2,1,0:T(1,128)} %reshape.382), calls=%async_computation | async-start | bytes 8192 | tf_op jit(solution)/shard_map/all_to_all | solution.py:200
where the time goes:
time: 151 us; the launch traced here: 149 us
  Pallas kernels  63.8 us (42%)
  waiting for transfers between devices  26.3 us (17%)
  other arithmetic  22.6 us (15%)
  starting transfers between devices  18.9 us (13%)
  local copies, waits for them, and re-layouts  17 us (11%)
    pallas_call x1, Pallas kernels, local_scores(): pl.pallas_call(filter_kernel, grid_spec=pltpu.PrefetchScalarGridSpec(num_...  63.8 us
    ppermute x7, waiting for transfers between devices, doubling(): other = lax.ppermute(x, axis, [(i, i ^ 1 << m) for i in range(size)])  20.4 us
    ppermute x7, starting transfers between devices, doubling(): other = lax.ppermute(x, axis, [(i, i ^ 1 << m) for i in range(size)])  14.5 us
    concatenate x6, other arithmetic, doubling(): x = jnp.concatenate([x, other], axis=0)  8.1 us
    all_to_all x1, waiting for transfers between devices, shards(): mine = lax.all_to_all(s, 'blk', 0, 0, tiled=True)  5.92 us
    all_to_all x1, starting transfers between devices, shards(): mine = lax.all_to_all(s, 'blk', 0, 0, tiled=True)  4.4 us
    unnamed x15, local copies, waits for them, and re-layouts  3.06 us
  transfers between devices with their start and end apart: 8, of which 5 were waited for; matrix products, arithmetic and copies ran while one was open for 17% of the time, Pallas kernels for 0%

commit v1 on v0

--- a/solution.py
+++ b/solution.py
@@ -147,8 +147,12 @@
         ],
         compiler_params=pltpu.CompilerParams(vmem_limit_bytes=56 * 1024 * 1024),
     )(idx, cnt, q_all, r2, qstack, bias_col, rtT)
-    col_pool = jnp.mean(col.reshape(tiles, qt_per, chunks, r4, cells), axis=-1)
-    row_pool = jnp.mean(row.reshape(tiles, qt_per, r4, chunks, cells), axis=-1)
+    hi = lax.Precision.HIGHEST
+    avg_c = (jnp.arange(CH)[:, None] // cells == jnp.arange(r4)[None, :]).astype(jnp.float32) / cells
+    col_pool = jnp.einsum("tpcl,lr->tpcr", col, avg_c, precision=hi)
+    avg_r = (jnp.arange(chunks * cells)[:, None] // cells == jnp.arange(chunks)[None, :]).astype(
+        jnp.float32) / cells
+    row_pool = jnp.einsum("tprl,lc->tprc", row, avg_r, precision=hi)
     row_pool = jnp.transpose(row_pool, (0, 1, 3, 2))
     packed = (0.5 * (row_pool + col_pool)).reshape(tiles, qt_per, nb, br)
     where_is = jnp.argsort(idx, axis=1)

time: 151 us -> 147 us (0.974)
  matrix products: 0 us -> 4.21 us
  local copies, waits for them, and re-layouts: 17 us -> 14.4 us
  Pallas kernels: 63.8 us -> 61.3 us
    dot_general x0 -> x2, matrix products: none -> 4.21 us  [the longest x1 2.79 us: local_scores(): col_pool = jnp.einsum('tpcl,lr->tpcr', col, avg_c, precision=hi)]
    pallas_call x1, Pallas kernels: 63.8 us -> 61.3 us  [local_scores(): pl.pallas_call(filter_kernel, grid_spec=pltpu.PrefetchScalarGridSpec(num_...]
    reshape x2 -> x0, local copies, waits for them, and re-layouts: 2.37 us -> none  [the longest x1 1.2 us: local_scores(): row_pool = jnp.mean(row.reshape(tiles, qt_per, r4, chunks, cells), axis=-1)]
  transfers between devices with their start and end apart: 8 -> 8, of which waited for: 5 -> 5; matrix products, arithmetic and copies ran while one was open for 17% -> 16% of each run, Pallas kernels for 0% -> 0%
where the time goes in v1:
time: 147 us; the launch traced here: 146 us
  Pallas kernels  61.3 us (42%)
  waiting for transfers between devices  26.1 us (18%)
  other arithmetic  21.1 us (14%)
  starting transfers between devices  19 us (13%)
  local copies, waits for them, and re-layouts  14.4 us (10%)
  matrix products  4.21 us (3%)
    pallas_call x1, Pallas kernels, local_scores(): pl.pallas_call(filter_kernel, grid_spec=pltpu.PrefetchScalarGridSpec(num_...  61.3 us
    ppermute x7, waiting for transfers between devices, doubling(): other = lax.ppermute(x, axis, [(i, i ^ 1 << m) for i in range(size)])  20.2 us
    ppermute x7, starting transfers between devices, doubling(): other = lax.ppermute(x, axis, [(i, i ^ 1 << m) for i in range(size)])  14.6 us
    concatenate x6, other arithmetic, doubling(): x = jnp.concatenate([x, other], axis=0)  7.3 us
    all_to_all x1, waiting for transfers between devices, shards(): mine = lax.all_to_all(s, 'blk', 0, 0, tiled=True)  5.92 us
    all_to_all x1, starting transfers between devices, shards(): mine = lax.all_to_all(s, 'blk', 0, 0, tiled=True)  4.36 us
    unnamed x15, local copies, waits for them, and re-layouts  3.06 us
  transfers between devices with their start and end apart: 8, of which 5 were waited for; matrix products, arithmetic and copies ran while one was open for 16% of the time, Pallas kernels for 0%

profile of v1, /device:TPU:0, one launch (start us, length us, event | category | flops | bytes accessed | tf_op | source)
XLA Modules:
  0.0 146.4 jit_solution(929508195037788523)
XLA Ops:
  0.0 1.0 fusion.8
  1.0 1.0 constant_dynamic-update-slice_fusion.4
  2.0 3.4 %collective-permute-start.3 = (bf16[2,64,512]{2,1,0:T(8,128)(2,1)S(1)}, bf16[2,64,512]{2,1,0:T(8,128)(2,1)}, u32[]{:S(2)}, u32[]{:S(2)}) collective-permute-start(bf16[2,64,512]{2,1,0:T(8,128)(2,1)S(1)} %get-tuple-element.32), channel_id=1, source_target_pairs={{0,64},{8,72},{16,80},{24,88},{32,96},{40,104},{48,112},{56,120},{... | collective-permute-start | bytes 393224 | tf_op jit(solution)/shard_map/ppermute | solution.py:165
  5.4 1.1 fusion.3
  6.5 1.1 fusion.4
  7.6 0.7 convert_element_type.43
  8.3 3.1 %collective-permute-start = (bf16[1,272,512]{2,1,0:T(8,128)(2,1)S(1)}, bf16[1,272,512]{2,1,0:T(8,128)(2,1)S(1)}, u32[]{:S(2)}, u32[]{:S(2)}) collective-permute-start(bf16[1,272,512]{2,1,0:T(8,128)(2,1)S(1)} %fusion.7), channel_id=1, source_target_pairs={{0,4},{1,5},{2,6},{3,7},{4,0},{5,1},{6,2},{7,3},{8,12},{9,13},{10,... | collective-permute-start | bytes 835592 | tf_op jit(solution)/shard_map/ppermute | solution.py:165
  11.6 1.2 sort.69
  12.9 0.7 convert_element_type.47
  13.5 0.7 convert_element_type.50
  14.3 1.0 sort.68
  15.3 2.1 %select_reduce_fusion = (bf16[16,64,64]{2,1,0:T(8,128)(2,1)}, bf16[16,64,64]{2,1,0:T(8,128)(2,1)}) fusion(f32[16,9]{1,0:T(8,128)S(1)} %convert_element_type.50, pred[9,64,64]{2,1,0:T(8,128)(4,1)S(1)} %fusion.5, f32[16,9]{1,0:T(8,128)S(1)} %convert_element_type.47), kind=kLoop, calls=%fused_computation.4 | loop fusion | flops 2228224 | bytes 300160 | tf_op jit(solution)/shard_map/reduce_sum | solution.py:26
  17.4 0.6 collective-permute-done
  18.0 1.6 %collective-permute-start.1 = (bf16[2,272,512]{2,1,0:T(8,128)(2,1)S(1)}, bf16[2,272,512]{2,1,0:T(8,128)(2,1)S(1)}, u32[]{:S(2)}, u32[]{:S(2)}) collective-permute-start(bf16[2,272,512]{2,1,0:T(8,128)(2,1)S(1)} %pad_maximum_fusion.3), channel_id=1, source_target_pairs={{0,2},{1,3},{2,0},{3,1},{4,6},{5,7},{6,4},{7,5},{8,10},{9,11},{10,... | collective-permute-start | bytes 1671176 | tf_op jit(solution)/shard_map/ppermute | solution.py:165
  19.6 1.6 %pad_maximum_fusion.5 = bf16[4,64,512]{2,1,0:T(8,128)(2,1)} fusion(bf16[2,64,512]{2,1,0:T(8,128)(2,1)} %collective-permute-done.3, bf16[2,64,512]{2,1,0:T(8,128)(2,1)S(1)} %get-tuple-element.32), kind=kLoop, calls=%fused_computation.28 | loop fusion | flops 131072 | bytes 524288 | tf_op jit(solution)/shard_map/concatenate | solution.py:166
  21.3 3.9 %collective-permute-start.4 = (bf16[4,64,512]{2,1,0:T(8,128)(2,1)}, bf16[4,64,512]{2,1,0:T(8,128)(2,1)S(1)}, u32[]{:S(2)}, u32[]{:S(2)}) collective-permute-start(bf16[4,64,512]{2,1,0:T(8,128)(2,1)} %pad_maximum_fusion.5), channel_id=1, source_target_pairs={{0,32},{8,40},{16,48},{24,56},{32,0},{40,8},{48,16},{56,24},{64,96... | collective-permute-start | bytes 786440 | tf_op jit(solution)/shard_map/ppermute | solution.py:165
  25.1 6.2 %collective-permute-done.1 = bf16[2,272,512]{2,1,0:T(8,128)(2,1)S(1)} collective-permute-done((bf16[2,272,512]{2,1,0:T(8,128)(2,1)S(1)}, bf16[2,272,512]{2,1,0:T(8,128)(2,1)S(1)}, u32[]{:S(2)}, u32[]{:S(2)}) %collective-permute-start.1) | collective-permute-done | bytes 557088 | tf_op jit(solution)/shard_map/ppermute | solution.py:165
  31.4 1.1 pad_maximum_fusion.1
  32.5 0.7 collective-permute-start.2
  33.1 1.8 %copy.32 = bf16[16,64,64]{1,2,0:T(8,128)(2,1)} copy(bf16[16,64,64]{2,1,0:T(8,128)(2,1)} %get-tuple-element.29) | data formatting | bytes 262144 | tf_op jit(solution)/shard_map/reduce_sum | solution.py:26
  35.0 1.3 broadcast_in_dim_reshape.5.bias_ref
  36.3 1.0 pad_maximum_fusion.4
  37.3 2.0 %collective-permute-start.5 = (bf16[8,64,512]{2,1,0:T(8,128)(2,1)S(1)}, bf16[8,64,512]{2,1,0:T(8,128)(2,1)S(1)}, u32[]{:S(2)}, u32[]{:S(2)}) collective-permute-start(bf16[8,64,512]{2,1,0:T(8,128)(2,1)S(1)} %pad_maximum_fusion.4), channel_id=1, source_target_pairs={{0,16},{8,24},{16,0},{24,8},{32,48},{40,56},{48,32},{56,40},{64,80... | collective-permute-start | bytes 1572872 | tf_op jit(solution)/shard_map/ppermute | solution.py:165
  39.4 0.9 constant_dynamic-update-slice_fusion.3
  40.3 8.7 %collective-permute-done.5 = bf16[8,64,512]{2,1,0:T(8,128)(2,1)S(1)} collective-permute-done((bf16[8,64,512]{2,1,0:T(8,128)(2,1)S(1)}, bf16[8,64,512]{2,1,0:T(8,128)(2,1)S(1)}, u32[]{:S(2)}, u32[]{:S(2)}) %collective-permute-start.5) | collective-permute-done | bytes 524320 | tf_op jit(solution)/shard_map/ppermute | solution.py:165
  49.0 2.0 %pad_maximum_fusion.2 = bf16[16,64,512]{2,1,0:T(8,128)(2,1)} fusion(bf16[8,64,512]{2,1,0:T(8,128)(2,1)S(1)} %collective-permute-done.5, bf16[4,64,512]{2,1,0:T(8,128)(2,1)S(1)} %collective-permute-done.4, bf16[2,64,512]{2,1,0:T(8,128)(2,1)} %collective-permute-done.3, bf16[2,64,512]{2,1,0:T(8,128)(2,1)} %copy-done.2), kind=kLoop, calls=%fused_computation.11 | loop fusion | flops 1572864 | bytes 2097152 | tf_op jit(solution)/shard_map/concatenate | solution.py:166
  51.1 1.3 copy-done.1
  52.4 4.7 %collective-permute-done.2 = bf16[4,272,512]{2,1,0:T(8,128)(2,1)} collective-permute-done((bf16[4,272,512]{2,1,0:T(8,128)(2,1)}, bf16[4,272,512]{2,1,0:T(8,128)(2,1)}, u32[]{:S(2)}, u32[]{:S(2)}) %collective-permute-start.2) | collective-permute-done | bytes 1114144 | tf_op jit(solution)/shard_map/ppermute | solution.py:165
  57.1 1.5 %pad_maximum_fusion.q_ref = bf16[8,272,512]{2,1,0:T(8,128)(2,1)S(1)} fusion(bf16[4,272,512]{2,1,0:T(8,128)(2,1)} %collective-permute-done.2, bf16[2,272,512]{2,1,0:T(8,128)(2,1)S(1)} %collective-permute-done.1, bf16[1,272,512]{2,1,0:T(8,128)(2,1)S(1)} %collective-permute-done, bf16[1,272,512]{2,1,0:T(8,128)(2,1)S(1)} %fusion.7), kind=kLoop, calls=%fused_computation.6 | loop fusion | flops 3342336 | bytes 4456448 | tf_op jit(solution)/shard_map/concatenate | solution.py:166
  58.7 0.6 gather_fusion
  59.3 0.6 convert_reduce_fusion
  59.9 0.7 sort.70
  60.6 0.7 copy.33.idx_ref
  61.2 0.7 sort.71
  62.1 2.3 %constant_dynamic-update-slice_fusion = bf16[32,64,512]{2,1,0:T(8,128)(2,1)} fusion(bf16[32,64,512]{2,1,0:T(8,128)(2,1)} %copy-done.1, bf16[16,64,512]{2,1,0:T(8,128)(2,1)} %collective-permute-done.6), kind=kLoop, calls=%fused_computation.49 | loop fusion | bytes 2097152 | tf_op jit(solution)/shard_map/concatenate | solution.py:166
  64.4 61.3 %shard_map.64 = (f32[8,4,8,256]{3,2,1,0:T(8,128)}, f32[8,4,4,512]{3,2,1,0:T(4,128)}) custom-call(s32[8,16]{1,0:T(8,128)} %copy.33.idx_ref, s32[8]{0:T(128)} %get-tuple-element.33.cnt_ref, bf16[8,272,512]{2,1,0:T(8,128)(2,1)} %copy-done, bf16[2048,512]{1,0:T(8,128)(2,1)} %bitcast.50, bf16[1024,64]{1,0:T(8,128)(2,1)} %bitcast.52, ...), custom_call_target="tpu_custom_call" | custom-call | tf_op jit(solution)/shard_map/pallas_call | solution.py:121
  125.7 2.8 %fusion.21 = f32[8,4,8,4]{2,3,1,0:T(4,128)S(1)} fusion(f32[8,4,8,256]{3,2,1,0:T(8,128)} %get-tuple-element.28, s32[256]{0:T(256)S(1)} %and_select_fusion), kind=kOutput, calls=%fused_computation.63 | convolution fusion | flops 3147776 | bytes 267264 | tf_op jit(solution)/shard_map/tpcl,lr->tpcr/dot_general | solution.py:152
  128.5 1.4 fusion.1
  130.0 0.3 copy.37
  130.3 0.9 gather_fusion.3
  131.6 0.6 gather_fusion.1
  132.3 0.6 gather_fusion.2
  133.0 0.7 reshape.450
  133.7 4.4 %all-to-all-start = ((f32[8,1,128]{2,1,0:T(1,128)}), f32[8,1,128]{2,1,0:T(1,128)S(1)}, u32[]{:S(2)}, u32[]{:S(2)}) async-start(f32[8,1,128]{2,1,0:T(1,128)} %reshape.450), calls=%async_computation | async-start | bytes 8192 | tf_op jit(solution)/shard_map/all_to_all | solution.py:204
  138.2 5.9 %all-to-all-done = f32[8,1,128]{2,1,0:T(1,128)S(1)} async-done(((f32[8,1,128]{2,1,0:T(1,128)}), f32[8,1,128]{2,1,0:T(1,128)S(1)}, u32[]{:S(2)}, u32[]{:S(2)}) %all-to-all-start) | async-done | bytes 4128 | tf_op jit(solution)/shard_map/all_to_all | solution.py:204
  144.2 0.5 broadcast.670
  144.7 0.7 reduce.3
  145.8 0.7 copy.41
  (61 shorter events, 2.1 us)
Async XLA Ops:
  2.0 17.6 %copy-start.2 = (bf16[2,64,512]{2,1,0:T(8,128)(2,1)}, bf16[2,64,512]{2,1,0:T(8,128)(2,1)S(1)}, u32[]{:S(2)}) copy-start(bf16[2,64,512]{2,1,0:T(8,128)(2,1)S(1)} %get-tuple-element.32) | copy-start | bytes 393220
  2.0 17.6 %collective-permute-start.3 = (bf16[2,64,512]{2,1,0:T(8,128)(2,1)S(1)}, bf16[2,64,512]{2,1,0:T(8,128)(2,1)}, u32[]{:S(2)}, u32[]{:S(2)}) collective-permute-start(bf16[2,64,512]{2,1,0:T(8,128)(2,1)S(1)} %get-tuple-element.32), channel_id=1, source_target_pairs={{0,64},{8,72},{16,80},{24,88},{32,96},{40,104},{48,112},{56,120},{... | collective-permute-start | bytes 393224 | tf_op jit(solution)/shard_map/ppermute | solution.py:165
  8.3 9.7 %collective-permute-start = (bf16[1,272,512]{2,1,0:T(8,128)(2,1)S(1)}, bf16[1,272,512]{2,1,0:T(8,128)(2,1)S(1)}, u32[]{:S(2)}, u32[]{:S(2)}) collective-permute-start(bf16[1,272,512]{2,1,0:T(8,128)(2,1)S(1)} %fusion.7), channel_id=1, source_target_pairs={{0,4},{1,5},{2,6},{3,7},{4,0},{5,1},{6,2},{7,3},{8,12},{9,13},{10,... | collective-permute-start | bytes 835592 | tf_op jit(solution)/shard_map/ppermute | solution.py:165
  17.4 17.5 %copy-start.3 = (f32[16]{0:T(128)S(1)}, f32[16]{0:T(128)}, u32[]{:S(2)}) copy-start(f32[16]{0:T(128)} %param.12) | copy-start | bytes 196
  18.0 13.3 %collective-permute-start.1 = (bf16[2,272,512]{2,1,0:T(8,128)(2,1)S(1)}, bf16[2,272,512]{2,1,0:T(8,128)(2,1)S(1)}, u32[]{:S(2)}, u32[]{:S(2)}) collective-permute-start(bf16[2,272,512]{2,1,0:T(8,128)(2,1)S(1)} %pad_maximum_fusion.3), channel_id=1, source_target_pairs={{0,2},{1,3},{2,0},{3,1},{4,6},{5,7},{6,4},{7,5},{8,10},{9,11},{10,... | collective-permute-start | bytes 1671176 | tf_op jit(solution)/shard_map/ppermute | solution.py:165
  21.3 15.0 %collective-permute-start.4 = (bf16[4,64,512]{2,1,0:T(8,128)(2,1)}, bf16[4,64,512]{2,1,0:T(8,128)(2,1)S(1)}, u32[]{:S(2)}, u32[]{:S(2)}) collective-permute-start(bf16[4,64,512]{2,1,0:T(8,128)(2,1)} %pad_maximum_fusion.5), channel_id=1, source_target_pairs={{0,32},{8,40},{16,48},{24,56},{32,0},{40,8},{48,16},{56,24},{64,96... | collective-permute-start | bytes 786440 | tf_op jit(solution)/shard_map/ppermute | solution.py:165
  32.5 24.6 %collective-permute-start.2 = (bf16[4,272,512]{2,1,0:T(8,128)(2,1)}, bf16[4,272,512]{2,1,0:T(8,128)(2,1)}, u32[]{:S(2)}, u32[]{:S(2)}) collective-permute-start(bf16[4,272,512]{2,1,0:T(8,128)(2,1)} %pad_maximum_fusion.1), channel_id=1, source_target_pairs={{0,1},{1,0},{2,3},{3,2},{4,5},{5,4},{6,7},{7,6},{8,9},{9,8},{10,11... | collective-permute-start | bytes 3342344 | tf_op jit(solution)/shard_map/ppermute | solution.py:165
  37.3 11.7 %collective-permute-start.5 = (bf16[8,64,512]{2,1,0:T(8,128)(2,1)S(1)}, bf16[8,64,512]{2,1,0:T(8,128)(2,1)S(1)}, u32[]{:S(2)}, u32[]{:S(2)}) collective-permute-start(bf16[8,64,512]{2,1,0:T(8,128)(2,1)S(1)} %pad_maximum_fusion.4), channel_id=1, source_target_pairs={{0,16},{8,24},{16,0},{24,8},{32,48},{40,56},{48,32},{56,40},{64,80... | collective-permute-start | bytes 1572872 | tf_op jit(solution)/shard_map/ppermute | solution.py:165
  51.0 11.1 %collective-permute-start.6 = (bf16[16,64,512]{2,1,0:T(8,128)(2,1)}, bf16[16,64,512]{2,1,0:T(8,128)(2,1)}, u32[]{:S(2)}, u32[]{:S(2)}) collective-permute-start(bf16[16,64,512]{2,1,0:T(8,128)(2,1)} %pad_maximum_fusion.2), channel_id=1, source_target_pairs={{0,8},{8,0},{16,24},{24,16},{32,40},{40,32},{48,56},{56,48},{64,72... | collective-permute-start | bytes 3145736 | tf_op jit(solution)/shard_map/ppermute | solution.py:165
  51.1 1.3 copy-start.1
  58.6 5.9 %copy-start = (bf16[8,272,512]{2,1,0:T(8,128)(2,1)}, bf16[8,272,512]{2,1,0:T(8,128)(2,1)S(1)}, u32[]{:S(2)}) copy-start(bf16[8,272,512]{2,1,0:T(8,128)(2,1)S(1)} %pad_maximum_fusion.q_ref) | copy-start | bytes 6684676
  125.7 12.4 %copy-start.4 = (s32[1,16]{1,0:T(1,128)S(1)}, s32[1,16]{1,0:T(1,128)}, u32[]{:S(2)}) copy-start(s32[1,16]{1,0:T(1,128)} %param.13) | copy-start | bytes 196
  133.7 10.5 %all-to-all-start = ((f32[8,1,128]{2,1,0:T(1,128)}), f32[8,1,128]{2,1,0:T(1,128)S(1)}, u32[]{:S(2)}, u32[]{:S(2)}) async-start(f32[8,1,128]{2,1,0:T(1,128)} %reshape.450), calls=%async_computation | async-start | bytes 8192 | tf_op jit(solution)/shard_map/all_to_all | solution.py:204

commit v2 on v1

--- a/solution.py
+++ b/solution.py
@@ -152,8 +152,7 @@
     col_pool = jnp.einsum("tpcl,lr->tpcr", col, avg_c, precision=hi)
     avg_r = (jnp.arange(chunks * cells)[:, None] // cells == jnp.arange(chunks)[None, :]).astype(
         jnp.float32) / cells
-    row_pool = jnp.einsum("tprl,lc->tprc", row, avg_r, precision=hi)
-    row_pool = jnp.transpose(row_pool, (0, 1, 3, 2))
+    row_pool = jnp.einsum("tprl,lc->tpcr", row, avg_r, precision=hi)
     packed = (0.5 * (row_pool + col_pool)).reshape(tiles, qt_per, nb, br)
     where_is = jnp.argsort(idx, axis=1)
     return jnp.take_along_axis(packed, where_is[:, None, :, None], axis=2)

time: 147 us -> 148 us (level)
  the two profiles are of different devices: /device:TPU:0 before, /device:TPU:80 now
where the time goes in v2:
time: 148 us; the launch traced here: 146 us
  Pallas kernels  61.1 us (41%)
  waiting for transfers between devices  29.2 us (20%)
  other arithmetic  21.1 us (14%)
  local copies, waits for them, and re-layouts  14.5 us (10%)
  starting transfers between devices  14.4 us (10%)
  matrix products  5.58 us (4%)
    pallas_call x1, Pallas kernels, local_scores(): pl.pallas_call(filter_kernel, grid_spec=pltpu.PrefetchScalarGridSpec(num_...  61.1 us
    ppermute x7, waiting for transfers between devices, doubling(): other = lax.ppermute(x, axis, [(i, i ^ 1 << m) for i in range(size)])  23.3 us
    ppermute x7, starting transfers between devices, doubling(): other = lax.ppermute(x, axis, [(i, i ^ 1 << m) for i in range(size)])  8.98 us
    concatenate x6, other arithmetic, doubling(): x = jnp.concatenate([x, other], axis=0)  7.3 us
    all_to_all x1, waiting for transfers between devices, shards(): mine = lax.all_to_all(s, 'blk', 0, 0, tiled=True)  5.92 us
    all_to_all x1, starting transfers between devices, shards(): mine = lax.all_to_all(s, 'blk', 0, 0, tiled=True)  5.46 us
    unnamed x15, local copies, waits for them, and re-layouts  3.06 us
  transfers between devices with their start and end apart: 8, of which 5 were waited for; matrix products, arithmetic and copies ran while one was open for 16% of the time, Pallas kernels for 0%

profile of v2, /device:TPU:80, one launch (start us, length us, event | category | flops | bytes accessed | tf_op | source)
XLA Modules:
  0.0 146.2 jit_solution(18171263619846988679)
XLA Ops:
  0.0 1.0 fusion.8
  1.0 1.0 constant_dynamic-update-slice_fusion.4
  2.0 0.4 collective-permute-start.3
  2.5 1.1 fusion.3
  3.5 1.1 fusion.4
  4.6 0.7 convert_element_type.43
  5.3 3.1 %collective-permute-start = (bf16[1,272,512]{2,1,0:T(8,128)(2,1)S(1)}, bf16[1,272,512]{2,1,0:T(8,128)(2,1)S(1)}, u32[]{:S(2)}, u32[]{:S(2)}) collective-permute-start(bf16[1,272,512]{2,1,0:T(8,128)(2,1)S(1)} %fusion.7), channel_id=1, source_target_pairs={{0,4},{1,5},{2,6},{3,7},{4,0},{5,1},{6,2},{7,3},{8,12},{9,13},{10,... | collective-permute-start | bytes 835592 | tf_op jit(solution)/shard_map/ppermute | solution.py:164
  8.6 1.2 sort.69
  9.9 0.7 convert_element_type.47
  10.6 0.7 convert_element_type.50
  11.3 1.0 sort.68
  12.3 2.1 %select_reduce_fusion = (bf16[16,64,64]{2,1,0:T(8,128)(2,1)}, bf16[16,64,64]{2,1,0:T(8,128)(2,1)}) fusion(f32[16,9]{1,0:T(8,128)S(1)} %convert_element_type.50, pred[9,64,64]{2,1,0:T(8,128)(4,1)S(1)} %fusion.5, f32[16,9]{1,0:T(8,128)S(1)} %convert_element_type.47), kind=kLoop, calls=%fused_computation.4 | loop fusion | flops 2228224 | bytes 300160 | tf_op jit(solution)/shard_map/reduce_sum | solution.py:26
  14.4 0.6 collective-permute-done
  15.1 1.6 %collective-permute-start.1 = (bf16[2,272,512]{2,1,0:T(8,128)(2,1)S(1)}, bf16[2,272,512]{2,1,0:T(8,128)(2,1)S(1)}, u32[]{:S(2)}, u32[]{:S(2)}) collective-permute-start(bf16[2,272,512]{2,1,0:T(8,128)(2,1)S(1)} %pad_maximum_fusion.3), channel_id=1, source_target_pairs={{0,2},{1,3},{2,0},{3,1},{4,6},{5,7},{6,4},{7,5},{8,10},{9,11},{10,... | collective-permute-start | bytes 1671176 | tf_op jit(solution)/shard_map/ppermute | solution.py:164
  16.7 1.6 %pad_maximum_fusion.5 = bf16[4,64,512]{2,1,0:T(8,128)(2,1)} fusion(bf16[2,64,512]{2,1,0:T(8,128)(2,1)} %collective-permute-done.3, bf16[2,64,512]{2,1,0:T(8,128)(2,1)S(1)} %get-tuple-element.32), kind=kLoop, calls=%fused_computation.28 | loop fusion | flops 131072 | bytes 524288 | tf_op jit(solution)/shard_map/concatenate | solution.py:165
  18.3 10.1 %collective-permute-done.1 = bf16[2,272,512]{2,1,0:T(8,128)(2,1)S(1)} collective-permute-done((bf16[2,272,512]{2,1,0:T(8,128)(2,1)S(1)}, bf16[2,272,512]{2,1,0:T(8,128)(2,1)S(1)}, u32[]{:S(2)}, u32[]{:S(2)}) %collective-permute-start.1) | collective-permute-done | bytes 557088 | tf_op jit(solution)/shard_map/ppermute | solution.py:164
  28.4 1.1 pad_maximum_fusion.1
  29.5 2.2 %collective-permute-start.2 = (bf16[4,272,512]{2,1,0:T(8,128)(2,1)}, bf16[4,272,512]{2,1,0:T(8,128)(2,1)}, u32[]{:S(2)}, u32[]{:S(2)}) collective-permute-start(bf16[4,272,512]{2,1,0:T(8,128)(2,1)} %pad_maximum_fusion.1), channel_id=1, source_target_pairs={{0,1},{1,0},{2,3},{3,2},{4,5},{5,4},{6,7},{7,6},{8,9},{9,8},{10,11... | collective-permute-start | bytes 3342344 | tf_op jit(solution)/shard_map/ppermute | solution.py:164
  31.7 1.8 %copy.34 = bf16[16,64,64]{1,2,0:T(8,128)(2,1)} copy(bf16[16,64,64]{2,1,0:T(8,128)(2,1)} %get-tuple-element.29) | data formatting | bytes 262144 | tf_op jit(solution)/shard_map/reduce_sum | solution.py:26
  33.5 1.3 broadcast_in_dim_reshape.5.bias_ref
  34.8 1.0 pad_maximum_fusion.4
  35.9 1.7 %collective-permute-start.5 = (bf16[8,64,512]{2,1,0:T(8,128)(2,1)S(1)}, bf16[8,64,512]{2,1,0:T(8,128)(2,1)S(1)}, u32[]{:S(2)}, u32[]{:S(2)}) collective-permute-start(bf16[8,64,512]{2,1,0:T(8,128)(2,1)S(1)} %pad_maximum_fusion.4), channel_id=1, source_target_pairs={{0,16},{8,24},{16,0},{24,8},{32,48},{40,56},{48,32},{56,40},{64,80... | collective-permute-start | bytes 1572872 | tf_op jit(solution)/shard_map/ppermute | solution.py:164
  37.6 0.9 constant_dynamic-update-slice_fusion.3
  38.5 8.8 %collective-permute-done.5 = bf16[8,64,512]{2,1,0:T(8,128)(2,1)S(1)} collective-permute-done((bf16[8,64,512]{2,1,0:T(8,128)(2,1)S(1)}, bf16[8,64,512]{2,1,0:T(8,128)(2,1)S(1)}, u32[]{:S(2)}, u32[]{:S(2)}) %collective-permute-start.5) | collective-permute-done | bytes 524320 | tf_op jit(solution)/shard_map/ppermute | solution.py:164
  47.4 2.0 %pad_maximum_fusion.2 = bf16[16,64,512]{2,1,0:T(8,128)(2,1)} fusion(bf16[8,64,512]{2,1,0:T(8,128)(2,1)S(1)} %collective-permute-done.5, bf16[4,64,512]{2,1,0:T(8,128)(2,1)S(1)} %collective-permute-done.4, bf16[2,64,512]{2,1,0:T(8,128)(2,1)} %collective-permute-done.3, bf16[2,64,512]{2,1,0:T(8,128)(2,1)} %copy-done.2), kind=kLoop, calls=%fused_computation.11 | loop fusion | flops 1572864 | bytes 2097152 | tf_op jit(solution)/shard_map/concatenate | solution.py:165
  49.5 1.3 copy-done.1
  50.8 3.8 %collective-permute-done.2 = bf16[4,272,512]{2,1,0:T(8,128)(2,1)} collective-permute-done((bf16[4,272,512]{2,1,0:T(8,128)(2,1)}, bf16[4,272,512]{2,1,0:T(8,128)(2,1)}, u32[]{:S(2)}, u32[]{:S(2)}) %collective-permute-start.2) | collective-permute-done | bytes 1114144 | tf_op jit(solution)/shard_map/ppermute | solution.py:164
  54.6 1.5 %pad_maximum_fusion.q_ref = bf16[8,272,512]{2,1,0:T(8,128)(2,1)S(1)} fusion(bf16[4,272,512]{2,1,0:T(8,128)(2,1)} %collective-permute-done.2, bf16[2,272,512]{2,1,0:T(8,128)(2,1)S(1)} %collective-permute-done.1, bf16[1,272,512]{2,1,0:T(8,128)(2,1)S(1)} %collective-permute-done, bf16[1,272,512]{2,1,0:T(8,128)(2,1)S(1)} %fusion.7), kind=kLoop, calls=%fused_computation.6 | loop fusion | flops 3342336 | bytes 4456448 | tf_op jit(solution)/shard_map/concatenate | solution.py:165
  56.1 0.6 gather_fusion
  56.7 0.6 convert_reduce_fusion
  57.3 0.7 sort.70
  58.0 0.7 copy.35.idx_ref
  58.7 0.7 sort.71
  59.6 2.3 %constant_dynamic-update-slice_fusion = bf16[32,64,512]{2,1,0:T(8,128)(2,1)} fusion(bf16[32,64,512]{2,1,0:T(8,128)(2,1)} %copy-done.1, bf16[16,64,512]{2,1,0:T(8,128)(2,1)} %collective-permute-done.6), kind=kLoop, calls=%fused_computation.50 | loop fusion | bytes 2097152 | tf_op jit(solution)/shard_map/concatenate | solution.py:165
  61.9 61.1 %shard_map.64 = (f32[8,4,8,256]{3,2,1,0:T(8,128)}, f32[8,4,4,512]{3,2,1,0:T(4,128)}) custom-call(s32[8,16]{1,0:T(8,128)} %copy.35.idx_ref, s32[8]{0:T(128)} %get-tuple-element.33.cnt_ref, bf16[8,272,512]{2,1,0:T(8,128)(2,1)} %copy-done, bf16[2048,512]{1,0:T(8,128)(2,1)} %bitcast.49, bf16[1024,64]{1,0:T(8,128)(2,1)} %bitcast.51, ...), custom_call_target="tpu_custom_call" | custom-call | tf_op jit(solution)/shard_map/pallas_call | solution.py:121
  123.0 2.8 %fusion.22 = f32[8,4,8,4]{2,3,1,0:T(4,128)S(1)} fusion(f32[8,4,8,256]{3,2,1,0:T(8,128)} %get-tuple-element.28, s32[256]{0:T(256)S(1)} %and_select_fusion), kind=kOutput, calls=%fused_computation.64 | convolution fusion | flops 3147776 | bytes 267264 | tf_op jit(solution)/shard_map/tpcl,lr->tpcr/dot_general | solution.py:152
  125.9 2.8 %fusion.1 = f32[8,4,8,4]{0,2,3,1:T(8,128)S(1)} fusion(f32[8,4,8,4]{0,2,3,1:T(8,128)S(1)} %copy.38, f32[8,4,4,512]{3,2,1,0:T(4,128)} %get-tuple-element.27, s32[512]{0:T(512)S(1)} %add_select_fusion), kind=kOutput, calls=%fused_computation.9 | convolution fusion | flops 6301696 | bytes 272384 | tf_op jit(solution)/shard_map/tprl,lc->tpcr/dot_general | solution.py:155
  128.7 0.3 copy.41
  129.0 0.9 gather_fusion.3
  130.0 0.3 copy.42
  130.3 0.6 gather_fusion.1
  131.0 0.6 gather_fusion.2
  131.7 0.7 reshape.450
  132.4 5.5 %all-to-all-start = ((f32[8,1,128]{2,1,0:T(1,128)}), f32[8,1,128]{2,1,0:T(1,128)S(1)}, u32[]{:S(2)}, u32[]{:S(2)}) async-start(f32[8,1,128]{2,1,0:T(1,128)} %reshape.450), calls=%async_computation | async-start | bytes 8192 | tf_op jit(solution)/shard_map/all_to_all | solution.py:203
  138.0 5.9 %all-to-all-done = f32[8,1,128]{2,1,0:T(1,128)S(1)} async-done(((f32[8,1,128]{2,1,0:T(1,128)}), f32[8,1,128]{2,1,0:T(1,128)S(1)}, u32[]{:S(2)}, u32[]{:S(2)}) %all-to-all-start) | async-done | bytes 4128 | tf_op jit(solution)/shard_map/all_to_all | solution.py:203
  144.0 0.5 broadcast.670
  144.5 0.7 reduce.3
  145.5 0.7 copy.45
  (62 shorter events, 1.8 us)
Async XLA Ops:
  2.0 14.6 %copy-start.2 = (bf16[2,64,512]{2,1,0:T(8,128)(2,1)}, bf16[2,64,512]{2,1,0:T(8,128)(2,1)S(1)}, u32[]{:S(2)}) copy-start(bf16[2,64,512]{2,1,0:T(8,128)(2,1)S(1)} %get-tuple-element.32) | copy-start | bytes 393220
  2.0 14.6 %collective-permute-start.3 = (bf16[2,64,512]{2,1,0:T(8,128)(2,1)S(1)}, bf16[2,64,512]{2,1,0:T(8,128)(2,1)}, u32[]{:S(2)}, u32[]{:S(2)}) collective-permute-start(bf16[2,64,512]{2,1,0:T(8,128)(2,1)S(1)} %get-tuple-element.32), channel_id=1, source_target_pairs={{0,64},{8,72},{16,80},{24,88},{32,96},{40,104},{48,112},{56,120},{... | collective-permute-start | bytes 393224 | tf_op jit(solution)/shard_map/ppermute | solution.py:164
  5.3 9.7 %collective-permute-start = (bf16[1,272,512]{2,1,0:T(8,128)(2,1)S(1)}, bf16[1,272,512]{2,1,0:T(8,128)(2,1)S(1)}, u32[]{:S(2)}, u32[]{:S(2)}) collective-permute-start(bf16[1,272,512]{2,1,0:T(8,128)(2,1)S(1)} %fusion.7), channel_id=1, source_target_pairs={{0,4},{1,5},{2,6},{3,7},{4,0},{5,1},{6,2},{7,3},{8,12},{9,13},{10,... | collective-permute-start | bytes 835592 | tf_op jit(solution)/shard_map/ppermute | solution.py:164
  14.4 19.0 %copy-start.3 = (f32[16]{0:T(128)S(1)}, f32[16]{0:T(128)}, u32[]{:S(2)}) copy-start(f32[16]{0:T(128)} %param.12) | copy-start | bytes 196
  15.1 13.3 %collective-permute-start.1 = (bf16[2,272,512]{2,1,0:T(8,128)(2,1)S(1)}, bf16[2,272,512]{2,1,0:T(8,128)(2,1)S(1)}, u32[]{:S(2)}, u32[]{:S(2)}) collective-permute-start(bf16[2,272,512]{2,1,0:T(8,128)(2,1)S(1)} %pad_maximum_fusion.3), channel_id=1, source_target_pairs={{0,2},{1,3},{2,0},{3,1},{4,6},{5,7},{6,4},{7,5},{8,10},{9,11},{10,... | collective-permute-start | bytes 1671176 | tf_op jit(solution)/shard_map/ppermute | solution.py:164
  18.3 16.5 %collective-permute-start.4 = (bf16[4,64,512]{2,1,0:T(8,128)(2,1)}, bf16[4,64,512]{2,1,0:T(8,128)(2,1)S(1)}, u32[]{:S(2)}, u32[]{:S(2)}) collective-permute-start(bf16[4,64,512]{2,1,0:T(8,128)(2,1)} %pad_maximum_fusion.5), channel_id=1, source_target_pairs={{0,32},{8,40},{16,48},{24,56},{32,0},{40,8},{48,16},{56,24},{64,96... | collective-permute-start | bytes 786440 | tf_op jit(solution)/shard_map/ppermute | solution.py:164
  29.5 25.1 %collective-permute-start.2 = (bf16[4,272,512]{2,1,0:T(8,128)(2,1)}, bf16[4,272,512]{2,1,0:T(8,128)(2,1)}, u32[]{:S(2)}, u32[]{:S(2)}) collective-permute-start(bf16[4,272,512]{2,1,0:T(8,128)(2,1)} %pad_maximum_fusion.1), channel_id=1, source_target_pairs={{0,1},{1,0},{2,3},{3,2},{4,5},{5,4},{6,7},{7,6},{8,9},{9,8},{10,11... | collective-permute-start | bytes 3342344 | tf_op jit(solution)/shard_map/ppermute | solution.py:164
  35.9 11.5 %collective-permute-start.5 = (bf16[8,64,512]{2,1,0:T(8,128)(2,1)S(1)}, bf16[8,64,512]{2,1,0:T(8,128)(2,1)S(1)}, u32[]{:S(2)}, u32[]{:S(2)}) collective-permute-start(bf16[8,64,512]{2,1,0:T(8,128)(2,1)S(1)} %pad_maximum_fusion.4), channel_id=1, source_target_pairs={{0,16},{8,24},{16,0},{24,8},{32,48},{40,56},{48,32},{56,40},{64,80... | collective-permute-start | bytes 1572872 | tf_op jit(solution)/shard_map/ppermute | solution.py:164
  49.4 10.2 %collective-permute-start.6 = (bf16[16,64,512]{2,1,0:T(8,128)(2,1)}, bf16[16,64,512]{2,1,0:T(8,128)(2,1)}, u32[]{:S(2)}, u32[]{:S(2)}) collective-permute-start(bf16[16,64,512]{2,1,0:T(8,128)(2,1)} %pad_maximum_fusion.2), channel_id=1, source_target_pairs={{0,8},{8,0},{16,24},{24,16},{32,40},{40,32},{48,56},{56,48},{64,72... | collective-permute-start | bytes 3145736 | tf_op jit(solution)/shard_map/ppermute | solution.py:164
  49.4 1.3 copy-start.1
  56.0 5.9 %copy-start = (bf16[8,272,512]{2,1,0:T(8,128)(2,1)}, bf16[8,272,512]{2,1,0:T(8,128)(2,1)S(1)}, u32[]{:S(2)}) copy-start(bf16[8,272,512]{2,1,0:T(8,128)(2,1)S(1)} %pad_maximum_fusion.q_ref) | copy-start | bytes 6684676
  123.0 14.9 %copy-start.4 = (s32[1,16]{1,0:T(1,128)S(1)}, s32[1,16]{1,0:T(1,128)}, u32[]{:S(2)}) copy-start(s32[1,16]{1,0:T(1,128)} %param.13) | copy-start | bytes 196
  132.4 11.6 %all-to-all-start = ((f32[8,1,128]{2,1,0:T(1,128)}), f32[8,1,128]{2,1,0:T(1,128)S(1)}, u32[]{:S(2)}, u32[]{:S(2)}) async-start(f32[8,1,128]{2,1,0:T(1,128)} %reshape.450), calls=%async_computation | async-start | bytes 8192 | tf_op jit(solution)/shard_map/all_to_all | solution.py:203
